TPU v7x, 32 devices: a whole 2x2x4 slice. The times are simulated.
32 devices in a mesh: seq: 16 (over z, y, core), dp: 2 (over x).
Axes of the slice: x: 2, y: 2, z: 4, core: 2. Of those that a mesh axis runs over, the one named last changes fastest.
Arguments:
- queries: bfloat16 [2, 3072, 1536], P('dp', 'seq'), may hold values from -100 to 100
- key_vectors: bfloat16 [2, 3072, 1536], P('dp', 'seq'), may hold values from -6 to 6
- value_vectors: bfloat16 [2, 3072, 1536], P('dp', 'seq'), may hold values from -48 to 48
- w_out: bfloat16 [1536, 1536], P(('seq', 'dp')), may hold values from -0.15625 to 0.15625
- cotangent: bfloat16 [2, 3072, 1536], P('dp', 'seq'), may hold values from -0.119628906 to 0.119628906
Outputs:
- projected: bfloat16 [2, 3072, 1536], P('dp', 'seq')
- grad_w_out: float32 [1536, 1536], P(('seq', 'dp'))
All inputs are finite; a program needn't handle non-finite values.
Results may differ from a plain program's by a relative error of at most 0.0055.
Values may be sent and summed in bfloat16 or wider, within the bound.
No kernel may reach another device: no remote copies, remote signals or barrier semaphores. Data moves between devices by JAX's collectives and lax.ppermute only.
A program may use at most 128 MiB of HBM per device.

v0:
```python
import jax
import jax.numpy as jnp
from jax import lax
from jax.sharding import Mesh
from jax.sharding import PartitionSpec as P

HEADS = 8
HEAD_DIM = 192


def attend(query_here, key_all, value_all):
    query_count = query_here.shape[0]
    head_width = query_here.shape[1]
    block_size = min(512, query_count)
    score_scale = HEAD_DIM ** (-0.5)

    def one_block(query_block):
        scores = jnp.dot(query_block, key_all.T, preferred_element_type=jnp.float32) * score_scale
        largest = jnp.max(scores, axis=1, keepdims=True)
        raised = jnp.exp(scores - largest)
        denominator = jnp.sum(raised, axis=1, keepdims=True)
        weights = raised.astype(jnp.bfloat16)
        mixed = jnp.dot(weights, value_all, preferred_element_type=jnp.float32)
        return (mixed / denominator).astype(jnp.bfloat16)

    blocks = lax.map(
        one_block, query_here.reshape(query_count // block_size, block_size, head_width)
    )
    return blocks.reshape(query_count, head_width)


ALL = ("side", "inner", "dp")


def local(queries, key_vectors, value_vectors, w_out, cotangent):
    head_count = HEADS
    head_width = HEAD_DIM
    side_count = lax.axis_size("side")
    dp_count = lax.axis_size("dp")
    row_count = queries.shape[1]
    width = queries.shape[2]
    dp_index = lax.axis_index("dp")
    w_full = lax.all_gather(w_out, ALL, axis=0, tiled=True)
    cot_side = lax.all_gather(cotangent[0], "inner", axis=0, tiled=True)

    def a2a(tensor):
        return lax.all_to_all(tensor, "inner", split_axis=0, concat_axis=0, tiled=True)

    def by_head(tensor):
        return tensor[0].reshape(row_count, head_count, head_width).transpose(1, 0, 2)

    side_index = lax.axis_index("side")

    def by_lane(tensor):
        return tensor[0].reshape(row_count, head_count, head_width)

    kv_raw = jnp.concatenate([by_lane(key_vectors), by_lane(value_vectors)], axis=2)
    inner_index = lax.axis_index("inner")
    kv_crossed = []
    for step in range(1, side_count):
        for shift in range(head_count):
            perm = [
                (
                    g * head_count + i,
                    (g + step) % side_count * head_count + (i + shift) % head_count,
                )
                for g in range(side_count)
                for i in range(head_count)
            ]
            outgoing = lax.dynamic_index_in_dim(
                kv_raw, (inner_index + shift) % head_count, axis=1, keepdims=False
            )
            kv_crossed.append(lax.ppermute(outgoing, ("side", "inner"), perm))
    stacked = jnp.concatenate([by_lane(queries), kv_raw], axis=2)
    got = lax.all_to_all(stacked, "inner", split_axis=1, concat_axis=0, tiled=True).reshape(
        head_count * row_count, 3 * head_width
    )
    early = len(kv_crossed)
    kv_early, got = lax.optimization_barrier((kv_crossed[:early], got))
    kv_crossed = list(kv_early) + kv_crossed[early:]
    query_here = got[:, :head_width]
    kv_all = jnp.concatenate([got[:, head_width:]] + kv_crossed, axis=0)
    key_all = kv_all[:, :head_width]
    value_all = kv_all[:, head_width:]
    attended_here = attend(query_here, key_all, value_all)
    partial = lax.dot_general(
        attended_here, cot_side, (((0,), (0,)), ((), ())), preferred_element_type=jnp.float32
    )
    returned = a2a(attended_here.reshape(head_count, row_count, head_width))
    attended = returned.transpose(1, 0, 2).reshape(row_count, width)
    projected = jnp.dot(attended, w_full, preferred_element_type=jnp.float32).astype(jnp.bfloat16)
    chunk_count = side_count * dp_count
    chunk = head_width // chunk_count
    side_index = lax.axis_index("side")
    if dp_count == 2:
        pieces = partial.reshape(side_count, dp_count, chunk, width)
        kept = lax.dynamic_index_in_dim(pieces, dp_index, axis=1, keepdims=False)
        sent = lax.dynamic_index_in_dim(pieces, 1 - dp_index, axis=1, keepdims=False)
        kept = kept + lax.ppermute(sent, "dp", [(0, 1), (1, 0)])
        grad_w_out = None
        for step in range(side_count):
            perm = []
            for g in range(side_count):
                for h in range(head_count):
                    for p in range(dp_count):
                        owner_side = (g + step) % side_count
                        source = (g * head_count + h) * dp_count + p
                        target = (side_count * h + owner_side) * dp_count + p
                        perm.append((source, target))
            outgoing = lax.dynamic_index_in_dim(
                kept, (side_index + step) % side_count, axis=0, keepdims=False
            )
            arrived = lax.ppermute(outgoing, ALL, perm)
            grad_w_out = arrived if grad_w_out is None else grad_w_out + arrived
    else:
        pieces = partial.reshape(chunk_count, chunk, width)
        holder = side_index * dp_count + dp_index
        grad_w_out = None
        for step in range(chunk_count):
            perm = []
            for g in range(side_count):
                for h in range(head_count):
                    for p in range(dp_count):
                        c = (g * dp_count + p + step) % chunk_count
                        source = (g * head_count + h) * dp_count + p
                        target = (side_count * h + c // dp_count) * dp_count + c % dp_count
                        perm.append((source, target))
            outgoing = lax.dynamic_index_in_dim(
                pieces, (holder + step) % chunk_count, axis=0, keepdims=False
            )
            arrived = lax.ppermute(outgoing, ALL, perm)
            grad_w_out = arrived if grad_w_out is None else grad_w_out + arrived
    return (projected.reshape(1, row_count, width), grad_w_out)


def solution(mesh):
    seq_count = mesh.shape["seq"]
    dp_count = mesh.shape["dp"]
    fine = Mesh(mesh.devices.reshape(seq_count // HEADS, HEADS, dp_count), ("side", "inner", "dp"))
    seq = ("side", "inner")
    placed = (
        P("dp", seq, None),
        P("dp", seq, None),
        P("dp", seq, None),
        P(ALL, None),
        P("dp", seq, None),
    )
    return jax.shard_map(
        local,
        mesh=fine,
        in_specs=placed,
        out_specs=(P("dp", seq, None), P(ALL, None)),
        check_vma=False,
    )
```

profile of v0, /device:TPU:1, one launch (start us, length us, event | category | flops | bytes accessed | tf_op | source)
XLA Modules:
  0.0 170.2 jit_solution(15018882049853274398)
XLA Ops:
  7.9 1.7 %reshape_squeeze.9 = bf16[192,8,192]{2,1,0:T(8,128)(2,1)S(1)} reshape(bf16[1,192,1536]{2,1,0:T(8,128)(2,1)} %param.8) | data formatting | bytes 1179648 | tf_op jit(solution)/shard_map/reshape;squeeze | solution.py:55
  11.5 2.0 %pad_maximum_fusion = bf16[192,8,576]{2,0,1:T(8,128)(2,1)} fusion(bf16[192,8,192]{2,0,1:T(8,128)(2,1)S(1)} %copy.13, bf16[192,8,192]{2,0,1:T(8,128)(2,1)S(1)} %copy.12, bf16[192,8,192]{2,0,1:T(8,128)(2,1)S(1)} %copy.14), kind=kLoop, calls=%fused_computation.20 | loop fusion | flops 5308416 | bytes 3538944 | tf_op jit(solution)/shard_map/concatenate | solution.py:74
  13.5 5.3 %all-to-all-start = ((bf16[192,8,576]{2,0,1:T(8,128)(2,1)}), bf16[192,8,576]{2,0,1:T(8,128)(2,1)S(1)}, u32[]{:S(2)}, u32[]{:S(2)}) async-start(bf16[192,8,576]{2,0,1:T(8,128)(2,1)} %pad_maximum_fusion), calls=%async_computation | async-start | bytes 3932160 | tf_op jit(solution)/shard_map/all_to_all | solution.py:75
  18.8 0.7 all-gather.4.cloned.1.call-update
  19.7 1.2 fusion.41
  20.9 2.3 %collective-permute-start = (bf16[192,384]{1,0:T(8,128)(2,1)}, bf16[192,384]{1,0:T(8,128)(2,1)}, u32[]{:S(2)}, u32[]{:S(2)}) collective-permute-start(bf16[192,384]{1,0:T(8,128)(2,1)} %get-tuple-element.63), channel_id=1, source_target_pairs={{0,16},{2,18},{4,20},{6,22},{8,24},{10,26},{12,28},{14,30},{16,0},... | collective-permute-start | bytes 442376 | tf_op jit(solution)/shard_map/ppermute | solution.py:73
  23.2 1.7 collective-permute-start.1
  24.9 2.3 %collective-permute-start.2 = (bf16[192,384]{1,0:T(8,128)(2,1)}, bf16[192,384]{1,0:T(8,128)(2,1)}, u32[]{:S(2)}, u32[]{:S(2)}) collective-permute-start(bf16[192,384]{1,0:T(8,128)(2,1)} %get-tuple-element.65), channel_id=1, source_target_pairs={{0,20},{2,22},{4,24},{6,26},{8,28},{10,30},{12,16},{14,18},{16,4},... | collective-permute-start | bytes 442376 | tf_op jit(solution)/shard_map/ppermute | solution.py:73
  27.2 1.2 collective-permute-start.3
  28.4 2.1 %collective-permute-start.4 = (bf16[192,384]{1,0:T(8,128)(2,1)}, bf16[192,384]{1,0:T(8,128)(2,1)}, u32[]{:S(2)}, u32[]{:S(2)}) collective-permute-start(bf16[192,384]{1,0:T(8,128)(2,1)} %get-tuple-element.67), channel_id=1, source_target_pairs={{0,24},{2,26},{4,28},{6,30},{8,16},{10,18},{12,20},{14,22},{16,8},... | collective-permute-start | bytes 442376 | tf_op jit(solution)/shard_map/ppermute | solution.py:73
  30.5 0.9 fusion.34
  31.4 30.7 %collective-permute-done = bf16[192,384]{1,0:T(8,128)(2,1)} collective-permute-done((bf16[192,384]{1,0:T(8,128)(2,1)}, bf16[192,384]{1,0:T(8,128)(2,1)}, u32[]{:S(2)}, u32[]{:S(2)}) %collective-permute-start) | collective-permute-done | bytes 147488 | tf_op jit(solution)/shard_map/ppermute | solution.py:73
  62.1 4.1 %collective-permute-start.7 = (bf16[192,384]{1,0:T(8,128)(2,1)}, bf16[192,384]{1,0:T(8,128)(2,1)S(1)}, u32[]{:S(2)}, u32[]{:S(2)}) collective-permute-start(bf16[192,384]{1,0:T(8,128)(2,1)} %get-tuple-element.62), channel_id=1, source_target_pairs={{0,30},{2,16},{4,18},{6,20},{8,22},{10,24},{12,26},{14,28},{16,14}... | collective-permute-start | bytes 442376 | tf_op jit(solution)/shard_map/ppermute | solution.py:73
  66.2 4.9 %collective-permute-start.5 = (bf16[192,384]{1,0:T(8,128)(2,1)}, bf16[192,384]{1,0:T(8,128)(2,1)S(1)}, u32[]{:S(2)}, u32[]{:S(2)}) collective-permute-start(bf16[192,384]{1,0:T(8,128)(2,1)} %get-tuple-element.69), channel_id=1, source_target_pairs={{0,26},{2,28},{4,30},{6,16},{8,18},{10,20},{12,22},{14,24},{16,10}... | collective-permute-start | bytes 442376 | tf_op jit(solution)/shard_map/ppermute | solution.py:73
  71.1 2.7 %collective-permute-done.2 = bf16[192,384]{1,0:T(8,128)(2,1)} collective-permute-done((bf16[192,384]{1,0:T(8,128)(2,1)}, bf16[192,384]{1,0:T(8,128)(2,1)}, u32[]{:S(2)}, u32[]{:S(2)}) %collective-permute-start.2) | collective-permute-done | bytes 147488 | tf_op jit(solution)/shard_map/ppermute | solution.py:73
  73.7 3.9 %collective-permute-done.3 = bf16[192,384]{1,0:T(8,128)(2,1)} collective-permute-done((bf16[192,384]{1,0:T(8,128)(2,1)}, bf16[192,384]{1,0:T(8,128)(2,1)}, u32[]{:S(2)}, u32[]{:S(2)}) %collective-permute-start.3) | collective-permute-done | bytes 147488 | tf_op jit(solution)/shard_map/ppermute | solution.py:73
  77.6 1.6 collective-permute-done.4
  79.2 13.2 %collective-permute-done.7 = bf16[192,384]{1,0:T(8,128)(2,1)S(1)} collective-permute-done((bf16[192,384]{1,0:T(8,128)(2,1)}, bf16[192,384]{1,0:T(8,128)(2,1)S(1)}, u32[]{:S(2)}, u32[]{:S(2)}) %collective-permute-start.7) | collective-permute-done | bytes 147488 | tf_op jit(solution)/shard_map/ppermute | solution.py:73
  92.4 7.3 %collective-permute-done.6 = bf16[192,384]{1,0:T(8,128)(2,1)S(1)} collective-permute-done((bf16[192,384]{1,0:T(8,128)(2,1)}, bf16[192,384]{1,0:T(8,128)(2,1)S(1)}, u32[]{:S(2)}, u32[]{:S(2)}) %collective-permute-start.6) | collective-permute-done | bytes 147488 | tf_op jit(solution)/shard_map/ppermute | solution.py:73
  100.9 0.9 constant_dynamic-update-slice_fusion.7
  101.8 0.9 constant_dynamic-update-slice_fusion.6
  102.7 0.9 constant_dynamic-update-slice_fusion.5
  103.7 0.9 constant_dynamic-update-slice_fusion.4
  104.6 0.9 constant_dynamic-update-slice_fusion.3
  105.7 1.9 %fusion.42 = (bf16[3072,192]{1,0:T(8,128)(2,1)}, bf16[3072,192]{1,0:T(8,128)(2,1)S(1)}) fusion(bf16[3072,384]{1,0:T(8,128)(2,1)S(1)} %constant_dynamic-update-slice_fusion), kind=kLoop, calls=%fused_computation.66 | loop fusion | bytes 4718592 | tf_op jit(solution)/shard_map/slice | solution.py:84
  107.6 12.0 %while.10 = (s32[]{:T(128)}, bf16[3,512,192]{1,2,0:T(8,128)(2,1)S(1)}, bf16[3,512,192]{2,1,0:T(8,128)(2,1)S(1)}, bf16[3072,192]{1,0:T(8,128)(2,1)S(1)}, bf16[3072,192]{1,0:T(8,128)(2,1)}, /*index=5*/s32[]{:T(128)}) while((s32[]{:T(128)}, bf16[3,512,192]{1,2,0:T(8,128)(2,1)S(1)}, bf16[3,512,192]{2,1,0:T(8,128)(2,1)S(1)}, ...), condition=%wide.region_3.4_spmd, body=%wide.region_0.3_spmd.sunk | while | flops 1220738048 | bytes 27207784 | solution.py:26
  107.6 1.1 multiply_reduce_fusion.2
  108.7 1.2 fusion.56
  110.1 1.5 fusion.57
  111.6 1.1 multiply_reduce_fusion.2
  112.7 1.2 fusion.56
  114.1 1.5 fusion.57
  115.6 1.1 multiply_reduce_fusion.2
  116.7 1.2 fusion.56
  118.1 1.5 fusion.57
  119.6 1.2 copy.17
  120.8 5.1 %all-to-all-start.1 = ((bf16[8,192,192]{2,1,0:T(8,128)(2,1)}), bf16[8,192,192]{2,1,0:T(8,128)(2,1)S(1)}, u32[]{:S(2)}, u32[]{:S(2)}) async-start(bf16[8,192,192]{2,1,0:T(8,128)(2,1)} %bitcast.14), calls=%async_computation.1 | async-start | bytes 1572864 | tf_op jit(solution)/shard_map/all_to_all | solution.py:47
  126.0 3.4 %fusion.23 = f32[2,2,48,1536]{3,2,1,0:T(8,128)S(1)} fusion(bf16[2,2,48,1536]{3,2,1,0:T(8,128)(2,1)S(1)} %bitcast.73, bf16[1,1536,1536]{2,1,0:T(8,128)(2,1)} %all-gather.6.cloned.1.call-done), kind=kOutput, calls=%fused_computation.16 | convolution fusion | flops 905969664 | bytes 6488064 | tf_op jit(solution)/shard_map/dot_general | solution.py:86
  129.4 1.3 collective-permute-start.8
  130.7 9.3 %all-to-all-done.1 = bf16[8,192,192]{2,1,0:T(8,128)(2,1)S(1)} async-done(((bf16[8,192,192]{2,1,0:T(8,128)(2,1)}), bf16[8,192,192]{2,1,0:T(8,128)(2,1)S(1)}, u32[]{:S(2)}, u32[]{:S(2)}) %all-to-all-start.1) | async-done | bytes 589856 | tf_op jit(solution)/shard_map/all_to_all | solution.py:47
  140.5 1.5 reshape.26
  142.0 2.5 %collective-permute-done.8 = f32[2,48,1536]{2,1,0:T(8,128)} collective-permute-done((f32[2,48,1536]{2,1,0:T(8,128)S(1)}, f32[2,48,1536]{2,1,0:T(8,128)}, u32[]{:S(2)}, u32[]{:S(2)}) %collective-permute-start.8) | collective-permute-done | bytes 589856 | tf_op jit(solution)/shard_map/ppermute | solution.py:99
  144.5 1.1 bitcast_add_fusion
  145.7 1.1 collective-permute-start.10
  146.8 3.4 %collective-permute-start.9 = (f32[48,1536]{1,0:T(8,128)S(1)}, f32[48,1536]{1,0:T(8,128)S(1)}, u32[]{:S(2)}, u32[]{:S(2)}) collective-permute-start(f32[48,1536]{1,0:T(8,128)S(1)} %get-tuple-element.71), channel_id=1, source_target_pairs={{0,0},{1,1},{2,4},{3,5},{4,8},{5,9},{6,12},{7,13},{8,16},{9,17},{1... | collective-permute-start | bytes 884744 | tf_op jit(solution)/shard_map/ppermute | solution.py:113
  150.2 4.2 %fusion.25 = bf16[1,192,1536]{2,1,0:T(8,128)(2,1)} fusion(bf16[192,1536]{1,0:T(8,128)(2,1)S(1)} %copy-done.3, bf16[1536,1536]{1,0:T(8,128)(2,1)} %all-gather.4.cloned.1.call-done), kind=kOutput, calls=%fused_computation.19 | convolution fusion | flops 906264576 | bytes 5898240 | tf_op jit(solution)/shard_map/dot_general | solution.py:91
  154.4 8.2 %collective-permute-done.9 = f32[48,1536]{1,0:T(8,128)S(1)} collective-permute-done((f32[48,1536]{1,0:T(8,128)S(1)}, f32[48,1536]{1,0:T(8,128)S(1)}, u32[]{:S(2)}, u32[]{:S(2)}) %collective-permute-start.9) | collective-permute-done | bytes 294944 | tf_op jit(solution)/shard_map/ppermute | solution.py:113
  162.6 0.7 add.135
  (45 shorter events, 5.1 us)
Async XLA Ops:
  7.2 2.7 %copy-start.1 = (bf16[1,192,1536]{2,1,0:T(8,128)(2,1)S(1)}, bf16[1,192,1536]{2,1,0:T(8,128)(2,1)}, u32[]{:S(2)}) copy-start(bf16[1,192,1536]{2,1,0:T(8,128)(2,1)} %param.9) | copy-start | bytes 1769476
  7.2 118.8 %all-gather.6.cloned.1.call-start = ((), (), s32[]{:S(2)}) async-start(), calls=%async_computation.3 | async-start | bytes 5308416 | tf_op jit(solution)/shard_map/all_gather | solution.py:44
  9.6 1.1 copy-start.2
  13.5 86.1 %all-to-all-start = ((bf16[192,8,576]{2,0,1:T(8,128)(2,1)}), bf16[192,8,576]{2,0,1:T(8,128)(2,1)S(1)}, u32[]{:S(2)}, u32[]{:S(2)}) async-start(bf16[192,8,576]{2,0,1:T(8,128)(2,1)} %pad_maximum_fusion), calls=%async_computation | async-start | bytes 3932160 | tf_op jit(solution)/shard_map/all_to_all | solution.py:75
  18.8 131.3 %all-gather.4.cloned.1.call-start = ((), (), s32[]{:S(2)}) async-start(), calls=%async_computation.2 | async-start | bytes 4866048 | tf_op jit(solution)/shard_map/all_gather | solution.py:43
  20.9 41.2 %collective-permute-start = (bf16[192,384]{1,0:T(8,128)(2,1)}, bf16[192,384]{1,0:T(8,128)(2,1)}, u32[]{:S(2)}, u32[]{:S(2)}) collective-permute-start(bf16[192,384]{1,0:T(8,128)(2,1)} %get-tuple-element.63), channel_id=1, source_target_pairs={{0,16},{2,18},{4,20},{6,22},{8,24},{10,26},{12,28},{14,30},{16,0},... | collective-permute-start | bytes 442376 | tf_op jit(solution)/shard_map/ppermute | solution.py:73
  23.2 43.0 %collective-permute-start.1 = (bf16[192,384]{1,0:T(8,128)(2,1)}, bf16[192,384]{1,0:T(8,128)(2,1)}, u32[]{:S(2)}, u32[]{:S(2)}) collective-permute-start(bf16[192,384]{1,0:T(8,128)(2,1)} %get-tuple-element.64), channel_id=1, source_target_pairs={{0,18},{2,20},{4,22},{6,24},{8,26},{10,28},{12,30},{14,16},{16,2},... | collective-permute-start | bytes 442376 | tf_op jit(solution)/shard_map/ppermute | solution.py:73
  24.9 48.8 %collective-permute-start.2 = (bf16[192,384]{1,0:T(8,128)(2,1)}, bf16[192,384]{1,0:T(8,128)(2,1)}, u32[]{:S(2)}, u32[]{:S(2)}) collective-permute-start(bf16[192,384]{1,0:T(8,128)(2,1)} %get-tuple-element.65), channel_id=1, source_target_pairs={{0,20},{2,22},{4,24},{6,26},{8,28},{10,30},{12,16},{14,18},{16,4},... | collective-permute-start | bytes 442376 | tf_op jit(solution)/shard_map/ppermute | solution.py:73
  27.2 50.4 %collective-permute-start.3 = (bf16[192,384]{1,0:T(8,128)(2,1)}, bf16[192,384]{1,0:T(8,128)(2,1)}, u32[]{:S(2)}, u32[]{:S(2)}) collective-permute-start(bf16[192,384]{1,0:T(8,128)(2,1)} %get-tuple-element.66), channel_id=1, source_target_pairs={{0,22},{2,24},{4,26},{6,28},{8,30},{10,16},{12,18},{14,20},{16,6},... | collective-permute-start | bytes 442376 | tf_op jit(solution)/shard_map/ppermute | solution.py:73
  28.4 50.8 %collective-permute-start.4 = (bf16[192,384]{1,0:T(8,128)(2,1)}, bf16[192,384]{1,0:T(8,128)(2,1)}, u32[]{:S(2)}, u32[]{:S(2)}) collective-permute-start(bf16[192,384]{1,0:T(8,128)(2,1)} %get-tuple-element.67), channel_id=1, source_target_pairs={{0,24},{2,26},{4,28},{6,30},{8,16},{10,18},{12,20},{14,22},{16,8},... | collective-permute-start | bytes 442376 | tf_op jit(solution)/shard_map/ppermute | solution.py:73
  62.1 30.3 %collective-permute-start.7 = (bf16[192,384]{1,0:T(8,128)(2,1)}, bf16[192,384]{1,0:T(8,128)(2,1)S(1)}, u32[]{:S(2)}, u32[]{:S(2)}) collective-permute-start(bf16[192,384]{1,0:T(8,128)(2,1)} %get-tuple-element.62), channel_id=1, source_target_pairs={{0,30},{2,16},{4,18},{6,20},{8,22},{10,24},{12,26},{14,28},{16,14}... | collective-permute-start | bytes 442376 | tf_op jit(solution)/shard_map/ppermute | solution.py:73
  66.2 26.2 %collective-permute-start.5 = (bf16[192,384]{1,0:T(8,128)(2,1)}, bf16[192,384]{1,0:T(8,128)(2,1)S(1)}, u32[]{:S(2)}, u32[]{:S(2)}) collective-permute-start(bf16[192,384]{1,0:T(8,128)(2,1)} %get-tuple-element.69), channel_id=1, source_target_pairs={{0,26},{2,28},{4,30},{6,16},{8,18},{10,20},{12,22},{14,24},{16,10}... | collective-permute-start | bytes 442376 | tf_op jit(solution)/shard_map/ppermute | solution.py:73
  73.7 25.9 %collective-permute-start.6 = (bf16[192,384]{1,0:T(8,128)(2,1)}, bf16[192,384]{1,0:T(8,128)(2,1)S(1)}, u32[]{:S(2)}, u32[]{:S(2)}) collective-permute-start(bf16[192,384]{1,0:T(8,128)(2,1)} %get-tuple-element.68), channel_id=1, source_target_pairs={{0,28},{2,30},{4,16},{6,18},{8,20},{10,22},{12,24},{14,26},{16,12}... | collective-permute-start | bytes 442376 | tf_op jit(solution)/shard_map/ppermute | solution.py:73
  92.4 7.3 %copy-start.4 = (bf16[192,384]{1,0:T(8,128)(2,1)}, bf16[192,384]{1,0:T(8,128)(2,1)S(1)}, u32[]{:S(2)}) copy-start(bf16[192,384]{1,0:T(8,128)(2,1)S(1)} %collective-permute-done.5) | copy-start | bytes 442372
  99.6 0.7 copy-start.6
  100.3 5.2 %copy-start.5 = (bf16[192,384]{1,0:T(8,128)(2,1)S(1)}, bf16[192,384]{1,0:T(8,128)(2,1)}, u32[]{:S(2)}) copy-start(bf16[192,384]{1,0:T(8,128)(2,1)} %copy-done.4) | copy-start | bytes 442372
  100.4 5.2 %copy-start.7 = (bf16[192,384]{1,0:T(8,128)(2,1)S(1)}, bf16[192,384]{1,0:T(8,128)(2,1)}, u32[]{:S(2)}) copy-start(bf16[192,384]{1,0:T(8,128)(2,1)} %copy-done.6) | copy-start | bytes 442372
  108.7 1.4 copy-start
  112.7 1.4 copy-start
  116.7 1.4 copy-start
  120.8 19.2 %all-to-all-start.1 = ((bf16[8,192,192]{2,1,0:T(8,128)(2,1)}), bf16[8,192,192]{2,1,0:T(8,128)(2,1)S(1)}, u32[]{:S(2)}, u32[]{:S(2)}) async-start(bf16[8,192,192]{2,1,0:T(8,128)(2,1)} %bitcast.14), calls=%async_computation.1 | async-start | bytes 1572864 | tf_op jit(solution)/shard_map/all_to_all | solution.py:47
  129.4 15.1 %collective-permute-start.8 = (f32[2,48,1536]{2,1,0:T(8,128)S(1)}, f32[2,48,1536]{2,1,0:T(8,128)}, u32[]{:S(2)}, u32[]{:S(2)}) collective-permute-start(f32[2,48,1536]{2,1,0:T(8,128)S(1)} %dynamic-slice_bitcast_fusion), channel_id=1, source_target_pairs={{0,1},{1,0},{2,3},{3,2},{4,5},{5,4},{6,7},{7,6},{8,9},{9,8},{10,11... | collective-permute-start | bytes 1769480 | tf_op jit(solution)/shard_map/ppermute | solution.py:99
  142.0 8.2 %copy-start.3 = (bf16[192,1536]{1,0:T(8,128)(2,1)S(1)}, bf16[192,1536]{1,0:T(8,128)(2,1)}, u32[]{:S(2)}) copy-start(bf16[192,1536]{1,0:T(8,128)(2,1)} %reshape.26) | copy-start | bytes 1769476
  145.7 8.7 %collective-permute-start.10 = (f32[48,1536]{1,0:T(8,128)S(1)}, f32[48,1536]{1,0:T(8,128)S(1)}, u32[]{:S(2)}, u32[]{:S(2)}) collective-permute-start(f32[48,1536]{1,0:T(8,128)S(1)} %get-tuple-element.70), channel_id=1, source_target_pairs={{0,2},{1,3},{2,6},{3,7},{4,10},{5,11},{6,14},{7,15},{8,18},{9,19},... | collective-permute-start | bytes 884744 | tf_op jit(solution)/shard_map/ppermute | solution.py:113
  146.8 15.8 %collective-permute-start.9 = (f32[48,1536]{1,0:T(8,128)S(1)}, f32[48,1536]{1,0:T(8,128)S(1)}, u32[]{:S(2)}, u32[]{:S(2)}) collective-permute-start(f32[48,1536]{1,0:T(8,128)S(1)} %get-tuple-element.71), channel_id=1, source_target_pairs={{0,0},{1,1},{2,4},{3,5},{4,8},{5,9},{6,12},{7,13},{8,16},{9,17},{1... | collective-permute-start | bytes 884744 | tf_op jit(solution)/shard_map/ppermute | solution.py:113
Sparse Core Ops, SparseCore 0:
  9.6 63.7 all-gather.5
  76.3 72.7 all-gather.3
where the time goes:
time: 171 us; the launch traced here: 170 us
  waiting for transfers between devices  80.7 us (47%)
  starting transfers between devices  34.8 us (20%)
  local copies, waits for them, and re-layouts  15.4 us (9%)
  matrix products  15.4 us (9%)
  between operations  14.3 us (8%)
  other arithmetic  9.51 us (6%)
    ppermute x8, waiting for transfers between devices, local(): kv_crossed.append(lax.ppermute(outgoing, ('side', 'inner'), perm))  59.3 us
    ppermute x8, starting transfers between devices, local(): kv_crossed.append(lax.ppermute(outgoing, ('side', 'inner'), perm))  18.6 us
    all_to_all x1, waiting for transfers between devices, a2a(): lax.all_to_all(tensor, 'inner', split_axis=0, concat_axis=0, tiled=True)  9.3 us
    ppermute x2, waiting for transfers between devices, local(): arrived = lax.ppermute(outgoing, ALL, perm)  8.16 us
    unnamed x22, local copies, waits for them, and re-layouts  6 us
    all_to_all x1, starting transfers between devices, local(): lax.all_to_all(stacked, 'inner', split_axis=1, concat_axis=0, tiled=True)  5.31 us
    all_to_all x1, starting transfers between devices, a2a(): lax.all_to_all(tensor, 'inner', split_axis=0, concat_axis=0, tiled=True)  5.14 us
    dot_general x3, matrix products, one_block(): mixed = jnp.dot(weights, value_all, preferred_element_type=jnp.float32)  4.42 us
  transfers between devices with their start and end apart: 15, of which 9 were waited for; matrix products, arithmetic and copies ran while one was open for 22% of the time, Pallas kernels for 0%

commit v1 on v0

--- a/solution.py
+++ b/solution.py
@@ -6,6 +6,13 @@
 
 HEADS = 8
 HEAD_DIM = 192
+
+
+def swap_blocks(array, axis, split, join):
+    size = lax.axis_size(axis)
+    blocks = jnp.stack(jnp.split(array, size, axis=split), axis=0)
+    blocks = lax.all_to_all(blocks, axis, split_axis=0, concat_axis=0)
+    return jnp.concatenate(blocks, axis=join)
 
 
 def attend(query_here, key_all, value_all):
@@ -72,9 +79,7 @@
             )
             kv_crossed.append(lax.ppermute(outgoing, ("side", "inner"), perm))
     stacked = jnp.concatenate([by_lane(queries), kv_raw], axis=2)
-    got = lax.all_to_all(stacked, "inner", split_axis=1, concat_axis=0, tiled=True).reshape(
-        head_count * row_count, 3 * head_width
-    )
+    got = swap_blocks(stacked, "inner", 1, 0).reshape(head_count * row_count, 3 * head_width)
     early = len(kv_crossed)
     kv_early, got = lax.optimization_barrier((kv_crossed[:early], got))
     kv_crossed = list(kv_early) + kv_crossed[early:]

time: 171 us -> 177 us (1.035)
  local copies, waits for them, and re-layouts: 15.4 us -> 30.1 us
  waiting for transfers between devices: 80.7 us -> 67.4 us
  other arithmetic: 9.51 us -> 13.1 us
  matrix products: 15.4 us -> 18.2 us
  starting transfers between devices: 34.8 us -> 32.7 us
    ppermute x8, waiting for transfers between devices: 59.3 us -> 46.1 us  [local(): kv_crossed.append(lax.ppermute(outgoing, ('side', 'inner'), perm))]
    unnamed x22 -> x29, local copies, waits for them, and re-layouts: 6 us -> 15.4 us
    concatenate x0 -> x2, other arithmetic: none -> 5.86 us  [local(): jnp.concatenate([by_lane(key_vectors), by_lane(value_vectors)], axis=2)]
    split x0 -> x1, local copies, waits for them, and re-layouts: none -> 3.29 us  [swap_blocks(): blocks = jnp.stack(jnp.split(array, size, axis=split), axis=0)]
    dot_general x3, matrix products: 3.32 us -> 6.15 us  [one_block(): jnp.dot(query_block, key_all.T, preferred_element_type=jnp.float32)]
    squeeze x2 -> x0, other arithmetic: 2.11 us -> none  [local(): lax.dynamic_index_in_dim(kv_raw, (inner_index + shift) % head_count, axis...]
    another operation x6 -> x3, local copies, waits for them, and re-layouts: 3.39 us -> 3.85 us  [by_lane(): return tensor[0].reshape(row_count, head_count, head_width)]
  transfers between devices with their start and end apart: 15 -> 15, of which waited for: 9 -> 9; matrix products, arithmetic and copies ran while one was open for 22% -> 34% of each run, Pallas kernels for 0% -> 0%
where the time goes in v1:
time: 177 us; the launch traced here: 176 us
  waiting for transfers between devices  67.4 us (38%)
  starting transfers between devices  32.7 us (18%)
  local copies, waits for them, and re-layouts  30.1 us (17%)
  matrix products  18.2 us (10%)
  between operations  14.3 us (8%)
  other arithmetic  13.1 us (7%)
    ppermute x8, waiting for transfers between devices, local(): kv_crossed.append(lax.ppermute(outgoing, ('side', 'inner'), perm))  46.1 us
    ppermute x8, starting transfers between devices, local(): kv_crossed.append(lax.ppermute(outgoing, ('side', 'inner'), perm))  17.5 us
    unnamed x29, local copies, waits for them, and re-layouts  15.4 us
    all_to_all x1, waiting for transfers between devices, a2a(): lax.all_to_all(tensor, 'inner', split_axis=0, concat_axis=0, tiled=True)  10.7 us
    ppermute x2, waiting for transfers between devices, local(): arrived = lax.ppermute(outgoing, ALL, perm)  8.09 us
    dot_general x3, matrix products, one_block(): jnp.dot(query_block, key_all.T, preferred_element_type=jnp.float32)  6.15 us
    concatenate x2, other arithmetic, local(): jnp.concatenate([by_lane(key_vectors), by_lane(value_vectors)], axis=2)  5.86 us
    all_to_all x1, starting transfers between devices, swap_blocks(): blocks = lax.all_to_all(blocks, axis, split_axis=0, concat_axis=0)  5.31 us
  transfers between devices with their start and end apart: 15, of which 9 were waited for; matrix products, arithmetic and copies ran while one was open for 34% of the time, Pallas kernels for 0%

profile of v1, /device:TPU:1, one launch (start us, length us, event | category | flops | bytes accessed | tf_op | source)
XLA Modules:
  0.0 176.0 jit_solution(14845971022519815148)
XLA Ops:
  7.9 1.7 reshape_squeeze.10
  10.3 1.5 reshape_squeeze.11
  11.8 1.9 %pad_maximum_fusion = bf16[192,8,576]{2,1,0:T(8,128)(2,1)S(1)} fusion(bf16[192,8,192]{2,1,0:T(8,128)(2,1)S(1)} %reshape_squeeze.10, bf16[192,8,192]{2,1,0:T(8,128)(2,1)S(1)} %reshape_squeeze.9, bf16[192,8,192]{2,1,0:T(8,128)(2,1)} %reshape_squeeze.11), kind=kLoop, calls=%fused_computation.20 | loop fusion | flops 5308416 | bytes 3538944 | tf_op jit(solution)/shard_map/concatenate | solution.py:81
  13.7 3.3 %fusion.35 = (bf16[192,1,576]{2,1,0:T(2,128)(2,1)S(1)}, bf16[192,1,576]{2,1,0:T(2,128)(2,1)S(1)}, bf16[192,1,576]{2,1,0:T(2,128)(2,1)S(1)}, bf16[192,1,576]{2,1,...) fusion(bf16[192,8,576]{2,1,0:T(8,128)(2,1)S(1)} %pad_maximum_fusion), kind=kLoop, calls=%fused_computation.75 | loop fusion | bytes 3538944 | tf_op jit(solution)/shard_map/split | solution.py:13
  22.8 5.3 %all-to-all-start = ((bf16[8,192,1,576]{3,1,2,0:T(8,128)(2,1)}), bf16[8,192,1,576]{3,1,2,0:T(8,128)(2,1)S(1)}, u32[]{:S(2)}, u32[]{:S(2)}) async-start(bf16[8,192,1,576]{3,1,2,0:T(8,128)(2,1)} %bitcast_dynamic-update-slice_fusion), calls=%async_computation | async-start | bytes 3932160 | tf_op jit(solution)/shard_map/all_to_all | solution.py:14
  28.9 4.7 %fusion.26 = (bf16[192,1,384]{2,1,0:T(2,128)(2,1)}, bf16[192,1,384]{2,1,0:T(2,128)(2,1)S(1)}, bf16[192,1,384]{2,1,0:T(2,128)(2,1)S(1)}, bf16[192,1,384]{2,1,0:T(...) fusion(s32[]{:T(128)S(6)} %select_n.97, bf16[192,8,192]{2,1,0:T(8,128)(2,1)S(1)} %reshape_squeeze.9, ...), kind=kLoop, calls=%fused_computation.40 | loop fusion | flops 1769472 | bytes 2064408 | tf_op jit(solution)/shard_map/concatenate | solution.py:64
  34.3 2.3 %collective-permute-start = (bf16[192,384]{1,0:T(8,128)(2,1)}, bf16[192,384]{1,0:T(8,128)(2,1)}, u32[]{:S(2)}, u32[]{:S(2)}) collective-permute-start(bf16[192,384]{1,0:T(8,128)(2,1)} %bitcast.80), channel_id=1, source_target_pairs={{0,16},{2,18},{4,20},{6,22},{8,24},{10,26},{12,28},{14,30},{16,0},... | collective-permute-start | bytes 442376 | tf_op jit(solution)/shard_map/ppermute | solution.py:80
  37.3 1.7 collective-permute-start.1
  39.7 2.3 %collective-permute-start.2 = (bf16[192,384]{1,0:T(8,128)(2,1)}, bf16[192,384]{1,0:T(8,128)(2,1)}, u32[]{:S(2)}, u32[]{:S(2)}) collective-permute-start(bf16[192,384]{1,0:T(8,128)(2,1)} %bitcast.78), channel_id=1, source_target_pairs={{0,20},{2,22},{4,24},{6,26},{8,28},{10,30},{12,16},{14,18},{16,4},... | collective-permute-start | bytes 442376 | tf_op jit(solution)/shard_map/ppermute | solution.py:80
  42.7 1.2 collective-permute-start.3
  44.6 2.1 %collective-permute-start.4 = (bf16[192,384]{1,0:T(8,128)(2,1)}, bf16[192,384]{1,0:T(8,128)(2,1)}, u32[]{:S(2)}, u32[]{:S(2)}) collective-permute-start(bf16[192,384]{1,0:T(8,128)(2,1)} %bitcast.76), channel_id=1, source_target_pairs={{0,24},{2,26},{4,28},{6,30},{8,16},{10,18},{12,20},{14,22},{16,8},... | collective-permute-start | bytes 442376 | tf_op jit(solution)/shard_map/ppermute | solution.py:80
  46.7 1.6 copy.126
  48.3 1.2 fusion.33
  49.5 14.4 %collective-permute-done = bf16[192,384]{1,0:T(8,128)(2,1)} collective-permute-done((bf16[192,384]{1,0:T(8,128)(2,1)}, bf16[192,384]{1,0:T(8,128)(2,1)}, u32[]{:S(2)}, u32[]{:S(2)}) %collective-permute-start) | collective-permute-done | bytes 147488 | tf_op jit(solution)/shard_map/ppermute | solution.py:80
  63.9 3.5 %collective-permute-start.7 = (bf16[192,384]{1,0:T(8,128)(2,1)}, bf16[192,384]{1,0:T(8,128)(2,1)S(1)}, u32[]{:S(2)}, u32[]{:S(2)}) collective-permute-start(bf16[192,384]{1,0:T(8,128)(2,1)} %bitcast.73), channel_id=1, source_target_pairs={{0,30},{2,16},{4,18},{6,20},{8,22},{10,24},{12,26},{14,28},{16,14}... | collective-permute-start | bytes 442376 | tf_op jit(solution)/shard_map/ppermute | solution.py:80
  67.4 4.4 %collective-permute-start.5 = (bf16[192,384]{1,0:T(8,128)(2,1)S(1)}, bf16[192,384]{1,0:T(8,128)(2,1)S(1)}, u32[]{:S(2)}, u32[]{:S(2)}) collective-permute-start(bf16[192,384]{1,0:T(8,128)(2,1)S(1)} %bitcast.96), channel_id=1, source_target_pairs={{0,26},{2,28},{4,30},{6,16},{8,18},{10,20},{12,22},{14,24},{16,10}... | collective-permute-start | bytes 442376 | tf_op jit(solution)/shard_map/ppermute | solution.py:80
  71.9 3.3 %collective-permute-done.2 = bf16[192,384]{1,0:T(8,128)(2,1)} collective-permute-done((bf16[192,384]{1,0:T(8,128)(2,1)}, bf16[192,384]{1,0:T(8,128)(2,1)}, u32[]{:S(2)}, u32[]{:S(2)}) %collective-permute-start.2) | collective-permute-done | bytes 147488 | tf_op jit(solution)/shard_map/ppermute | solution.py:80
  75.1 3.3 %collective-permute-done.3 = bf16[192,384]{1,0:T(8,128)(2,1)} collective-permute-done((bf16[192,384]{1,0:T(8,128)(2,1)}, bf16[192,384]{1,0:T(8,128)(2,1)}, u32[]{:S(2)}, u32[]{:S(2)}) %collective-permute-start.3) | collective-permute-done | bytes 147488 | tf_op jit(solution)/shard_map/ppermute | solution.py:80
  78.4 1.8 %collective-permute-done.4 = bf16[192,384]{1,0:T(8,128)(2,1)} collective-permute-done((bf16[192,384]{1,0:T(8,128)(2,1)}, bf16[192,384]{1,0:T(8,128)(2,1)}, u32[]{:S(2)}, u32[]{:S(2)}) %collective-permute-start.4) | collective-permute-done | bytes 147488 | tf_op jit(solution)/shard_map/ppermute | solution.py:80
  80.2 16.7 %collective-permute-done.7 = bf16[192,384]{1,0:T(8,128)(2,1)S(1)} collective-permute-done((bf16[192,384]{1,0:T(8,128)(2,1)}, bf16[192,384]{1,0:T(8,128)(2,1)S(1)}, u32[]{:S(2)}, u32[]{:S(2)}) %collective-permute-start.7) | collective-permute-done | bytes 147488 | tf_op jit(solution)/shard_map/ppermute | solution.py:80
  96.9 6.7 %collective-permute-done.6 = bf16[192,384]{1,0:T(8,128)(2,1)S(1)} collective-permute-done((bf16[192,384]{1,0:T(8,128)(2,1)S(1)}, bf16[192,384]{1,0:T(8,128)(2,1)S(1)}, u32[]{:S(2)}, u32[]{:S(2)}) %collective-permute-start.6) | collective-permute-done | bytes 147488 | tf_op jit(solution)/shard_map/ppermute | solution.py:80
  104.9 0.9 constant_dynamic-update-slice_fusion.7
  105.9 0.9 constant_dynamic-update-slice_fusion.6
  106.8 0.9 constant_dynamic-update-slice_fusion.5
  107.7 0.9 constant_dynamic-update-slice_fusion.4
  109.7 1.9 %fusion.34 = (bf16[3072,192]{1,0:T(8,128)(2,1)}, bf16[3072,192]{1,0:T(8,128)(2,1)S(1)}) fusion(bf16[3072,384]{1,0:T(8,128)(2,1)S(1)} %constant_dynamic-update-slice_fusion), kind=kLoop, calls=%fused_computation.74 | loop fusion | bytes 4718592 | tf_op jit(solution)/shard_map/slice | solution.py:89
  111.6 14.9 %while.10 = (s32[]{:T(128)}, bf16[3,512,192]{1,2,0:T(8,128)(2,1)S(1)}, bf16[3,512,192]{2,1,0:T(8,128)(2,1)}, bf16[3072,192]{1,0:T(8,128)(2,1)S(1)}, bf16[3072,192]{1,0:T(8,128)(2,1)}, /*index=5*/s32[]{:T(128)}) while((s32[]{:T(128)}, bf16[3,512,192]{1,2,0:T(8,128)(2,1)S(1)}, bf16[3,512,192]{2,1,0:T(8,128)(2,1)}, ...), condition=%wide.region_3.4_spmd, body=%wide.region_0.3_spmd.sunk | while | flops 1220738048 | bytes 26815076 | solution.py:33
  111.6 2.0 %multiply_reduce_fusion.2 = (f32[512]{0:T(512)S(1)}, f32[512,3072]{1,0:T(8,128)S(1)}) fusion(bf16[3072,192]{1,0:T(8,128)(2,1)S(1)} %get-tuple-element.130, bf16[3,512,192]{2,1,0:T(8,128)(2,1)} %get-tuple-element.129, s32[]{:T(128)} %get-tuple-element.121), kind=kOutput, calls=%fused_computation.1.clone.1 | convolution fusion | flops 607124992 | bytes 7735808 | tf_op jit(solution)/shard_map/while/body/eval_jaxpr/dot_general | solution.py:25
  113.7 1.2 fusion.49
  115.1 1.5 fusion.50
  116.6 2.1 %multiply_reduce_fusion.2 = (f32[512]{0:T(512)S(1)}, f32[512,3072]{1,0:T(8,128)S(1)}) fusion(bf16[3072,192]{1,0:T(8,128)(2,1)S(1)} %get-tuple-element.130, bf16[3,512,192]{2,1,0:T(8,128)(2,1)} %get-tuple-element.129, s32[]{:T(128)} %get-tuple-element.121), kind=kOutput, calls=%fused_computation.1.clone.1 | convolution fusion | flops 607124992 | bytes 7735808 | tf_op jit(solution)/shard_map/while/body/eval_jaxpr/dot_general | solution.py:25
  118.6 1.2 fusion.49
  120.1 1.5 fusion.50
  121.5 2.1 %multiply_reduce_fusion.2 = (f32[512]{0:T(512)S(1)}, f32[512,3072]{1,0:T(8,128)S(1)}) fusion(bf16[3072,192]{1,0:T(8,128)(2,1)S(1)} %get-tuple-element.130, bf16[3,512,192]{2,1,0:T(8,128)(2,1)} %get-tuple-element.129, s32[]{:T(128)} %get-tuple-element.121), kind=kOutput, calls=%fused_computation.1.clone.1 | convolution fusion | flops 607124992 | bytes 7735808 | tf_op jit(solution)/shard_map/while/body/eval_jaxpr/dot_general | solution.py:25
  123.6 1.2 fusion.49
  125.0 1.5 fusion.50
  126.5 1.2 copy.89
  127.7 4.0 %all-to-all-start.1 = ((bf16[8,192,192]{2,1,0:T(8,128)(2,1)}), bf16[8,192,192]{2,1,0:T(8,128)(2,1)S(1)}, u32[]{:S(2)}, u32[]{:S(2)}) async-start(bf16[8,192,192]{2,1,0:T(8,128)(2,1)} %bitcast.4), calls=%async_computation.1 | async-start | bytes 1572864 | tf_op jit(solution)/shard_map/all_to_all | solution.py:54
  131.7 3.4 %fusion.23 = f32[2,2,48,1536]{3,2,1,0:T(8,128)S(1)} fusion(bf16[2,2,48,1536]{3,2,1,0:T(8,128)(2,1)S(1)} %bitcast.93, bf16[1,1536,1536]{2,1,0:T(8,128)(2,1)} %all-gather.6.cloned.1.call-done), kind=kOutput, calls=%fused_computation.16 | convolution fusion | flops 905969664 | bytes 6488064 | tf_op jit(solution)/shard_map/dot_general | solution.py:91
  135.2 1.2 collective-permute-start.8
  136.4 10.7 %all-to-all-done.1 = bf16[8,192,192]{2,1,0:T(8,128)(2,1)S(1)} async-done(((bf16[8,192,192]{2,1,0:T(8,128)(2,1)}), bf16[8,192,192]{2,1,0:T(8,128)(2,1)S(1)}, u32[]{:S(2)}, u32[]{:S(2)}) %all-to-all-start.1) | async-done | bytes 589856 | tf_op jit(solution)/shard_map/all_to_all | solution.py:54
  147.6 1.5 reshape.21
  149.1 1.1 collective-permute-done.8
  150.2 1.1 bitcast_add_fusion
  151.4 1.2 collective-permute-start.10
  152.5 3.5 %collective-permute-start.9 = (f32[48,1536]{1,0:T(8,128)S(1)}, f32[48,1536]{1,0:T(8,128)S(1)}, u32[]{:S(2)}, u32[]{:S(2)}) collective-permute-start(f32[48,1536]{1,0:T(8,128)S(1)} %get-tuple-element.79), channel_id=1, source_target_pairs={{0,0},{1,1},{2,4},{3,5},{4,8},{5,9},{6,12},{7,13},{8,16},{9,17},{1... | collective-permute-start | bytes 884744 | tf_op jit(solution)/shard_map/ppermute | solution.py:118
  156.1 4.2 %fusion.25 = bf16[1,192,1536]{2,1,0:T(8,128)(2,1)} fusion(bf16[192,1536]{1,0:T(8,128)(2,1)S(1)} %copy-done.3, bf16[1536,1536]{1,0:T(8,128)(2,1)} %all-gather.4.cloned.1.call-done), kind=kOutput, calls=%fused_computation.19 | convolution fusion | flops 906264576 | bytes 5898240 | tf_op jit(solution)/shard_map/dot_general | solution.py:96
  160.3 8.1 %collective-permute-done.9 = f32[48,1536]{1,0:T(8,128)S(1)} collective-permute-done((f32[48,1536]{1,0:T(8,128)S(1)}, f32[48,1536]{1,0:T(8,128)S(1)}, u32[]{:S(2)}, u32[]{:S(2)}) %collective-permute-start.9) | collective-permute-done | bytes 294944 | tf_op jit(solution)/shard_map/ppermute | solution.py:118
  (51 shorter events, 15.8 us)
Async XLA Ops:
  7.2 2.5 %copy-start.1 = (bf16[1,192,1536]{2,1,0:T(8,128)(2,1)S(1)}, bf16[1,192,1536]{2,1,0:T(8,128)(2,1)}, u32[]{:S(2)}) copy-start(bf16[1,192,1536]{2,1,0:T(8,128)(2,1)} %param.8) | copy-start | bytes 1769476
  7.2 3.1 %copy-start.2 = (bf16[1,192,1536]{2,1,0:T(8,128)(2,1)S(1)}, bf16[1,192,1536]{2,1,0:T(8,128)(2,1)}, u32[]{:S(2)}) copy-start(bf16[1,192,1536]{2,1,0:T(8,128)(2,1)} %param.7) | copy-start | bytes 1769476
  7.2 124.5 %all-gather.6.cloned.1.call-start = ((), (), s32[]{:S(2)}) async-start(), calls=%async_computation.3 | async-start | bytes 5308416 | tf_op jit(solution)/shard_map/all_gather | solution.py:51
  22.8 80.7 %all-to-all-start = ((bf16[8,192,1,576]{3,1,2,0:T(8,128)(2,1)}), bf16[8,192,1,576]{3,1,2,0:T(8,128)(2,1)S(1)}, u32[]{:S(2)}, u32[]{:S(2)}) async-start(bf16[8,192,1,576]{3,1,2,0:T(8,128)(2,1)} %bitcast_dynamic-update-slice_fusion), calls=%async_computation | async-start | bytes 3932160 | tf_op jit(solution)/shard_map/all_to_all | solution.py:14
  28.1 127.9 %all-gather.4.cloned.1.call-start = ((), (), s32[]{:S(2)}) async-start(), calls=%async_computation.2 | async-start | bytes 4866048 | tf_op jit(solution)/shard_map/all_gather | solution.py:50
  34.3 29.6 %collective-permute-start = (bf16[192,384]{1,0:T(8,128)(2,1)}, bf16[192,384]{1,0:T(8,128)(2,1)}, u32[]{:S(2)}, u32[]{:S(2)}) collective-permute-start(bf16[192,384]{1,0:T(8,128)(2,1)} %bitcast.80), channel_id=1, source_target_pairs={{0,16},{2,18},{4,20},{6,22},{8,24},{10,26},{12,28},{14,30},{16,0},... | collective-permute-start | bytes 442376 | tf_op jit(solution)/shard_map/ppermute | solution.py:80
  37.3 30.1 %collective-permute-start.1 = (bf16[192,384]{1,0:T(8,128)(2,1)}, bf16[192,384]{1,0:T(8,128)(2,1)}, u32[]{:S(2)}, u32[]{:S(2)}) collective-permute-start(bf16[192,384]{1,0:T(8,128)(2,1)} %bitcast.79), channel_id=1, source_target_pairs={{0,18},{2,20},{4,22},{6,24},{8,26},{10,28},{12,30},{14,16},{16,2},... | collective-permute-start | bytes 442376 | tf_op jit(solution)/shard_map/ppermute | solution.py:80
  39.7 35.4 %collective-permute-start.2 = (bf16[192,384]{1,0:T(8,128)(2,1)}, bf16[192,384]{1,0:T(8,128)(2,1)}, u32[]{:S(2)}, u32[]{:S(2)}) collective-permute-start(bf16[192,384]{1,0:T(8,128)(2,1)} %bitcast.78), channel_id=1, source_target_pairs={{0,20},{2,22},{4,24},{6,26},{8,28},{10,30},{12,16},{14,18},{16,4},... | collective-permute-start | bytes 442376 | tf_op jit(solution)/shard_map/ppermute | solution.py:80
  42.7 35.7 %collective-permute-start.3 = (bf16[192,384]{1,0:T(8,128)(2,1)}, bf16[192,384]{1,0:T(8,128)(2,1)}, u32[]{:S(2)}, u32[]{:S(2)}) collective-permute-start(bf16[192,384]{1,0:T(8,128)(2,1)} %bitcast.77), channel_id=1, source_target_pairs={{0,22},{2,24},{4,26},{6,28},{8,30},{10,16},{12,18},{14,20},{16,6},... | collective-permute-start | bytes 442376 | tf_op jit(solution)/shard_map/ppermute | solution.py:80
  44.6 35.6 %collective-permute-start.4 = (bf16[192,384]{1,0:T(8,128)(2,1)}, bf16[192,384]{1,0:T(8,128)(2,1)}, u32[]{:S(2)}, u32[]{:S(2)}) collective-permute-start(bf16[192,384]{1,0:T(8,128)(2,1)} %bitcast.76), channel_id=1, source_target_pairs={{0,24},{2,26},{4,28},{6,30},{8,16},{10,18},{12,20},{14,22},{16,8},... | collective-permute-start | bytes 442376 | tf_op jit(solution)/shard_map/ppermute | solution.py:80
  63.9 32.9 %collective-permute-start.7 = (bf16[192,384]{1,0:T(8,128)(2,1)}, bf16[192,384]{1,0:T(8,128)(2,1)S(1)}, u32[]{:S(2)}, u32[]{:S(2)}) collective-permute-start(bf16[192,384]{1,0:T(8,128)(2,1)} %bitcast.73), channel_id=1, source_target_pairs={{0,30},{2,16},{4,18},{6,20},{8,22},{10,24},{12,26},{14,28},{16,14}... | collective-permute-start | bytes 442376 | tf_op jit(solution)/shard_map/ppermute | solution.py:80
  67.4 29.4 %collective-permute-start.5 = (bf16[192,384]{1,0:T(8,128)(2,1)S(1)}, bf16[192,384]{1,0:T(8,128)(2,1)S(1)}, u32[]{:S(2)}, u32[]{:S(2)}) collective-permute-start(bf16[192,384]{1,0:T(8,128)(2,1)S(1)} %bitcast.96), channel_id=1, source_target_pairs={{0,26},{2,28},{4,30},{6,16},{8,18},{10,20},{12,22},{14,24},{16,10}... | collective-permute-start | bytes 442376 | tf_op jit(solution)/shard_map/ppermute | solution.py:80
  75.1 28.4 %collective-permute-start.6 = (bf16[192,384]{1,0:T(8,128)(2,1)S(1)}, bf16[192,384]{1,0:T(8,128)(2,1)S(1)}, u32[]{:S(2)}, u32[]{:S(2)}) collective-permute-start(bf16[192,384]{1,0:T(8,128)(2,1)S(1)} %bitcast.95), channel_id=1, source_target_pairs={{0,28},{2,30},{4,16},{6,18},{8,20},{10,22},{12,24},{14,26},{16,12}... | collective-permute-start | bytes 442376 | tf_op jit(solution)/shard_map/ppermute | solution.py:80
  113.7 1.4 copy-start
  118.6 1.4 copy-start
  123.6 1.4 copy-start
  127.7 19.4 %all-to-all-start.1 = ((bf16[8,192,192]{2,1,0:T(8,128)(2,1)}), bf16[8,192,192]{2,1,0:T(8,128)(2,1)S(1)}, u32[]{:S(2)}, u32[]{:S(2)}) async-start(bf16[8,192,192]{2,1,0:T(8,128)(2,1)} %bitcast.4), calls=%async_computation.1 | async-start | bytes 1572864 | tf_op jit(solution)/shard_map/all_to_all | solution.py:54
  135.2 15.0 %collective-permute-start.8 = (f32[2,48,1536]{2,1,0:T(8,128)S(1)}, f32[2,48,1536]{2,1,0:T(8,128)}, u32[]{:S(2)}, u32[]{:S(2)}) collective-permute-start(f32[2,48,1536]{2,1,0:T(8,128)S(1)} %dynamic-slice_bitcast_fusion), channel_id=1, source_target_pairs={{0,1},{1,0},{2,3},{3,2},{4,5},{5,4},{6,7},{7,6},{8,9},{9,8},{10,11... | collective-permute-start | bytes 1769480 | tf_op jit(solution)/shard_map/ppermute | solution.py:104
  149.1 7.0 %copy-start.3 = (bf16[192,1536]{1,0:T(8,128)(2,1)S(1)}, bf16[192,1536]{1,0:T(8,128)(2,1)}, u32[]{:S(2)}) copy-start(bf16[192,1536]{1,0:T(8,128)(2,1)} %reshape.21) | copy-start | bytes 1769476
  151.4 9.0 %collective-permute-start.10 = (f32[48,1536]{1,0:T(8,128)S(1)}, f32[48,1536]{1,0:T(8,128)S(1)}, u32[]{:S(2)}, u32[]{:S(2)}) collective-permute-start(f32[48,1536]{1,0:T(8,128)S(1)} %get-tuple-element.78), channel_id=1, source_target_pairs={{0,2},{1,3},{2,6},{3,7},{4,10},{5,11},{6,14},{7,15},{8,18},{9,19},... | collective-permute-start | bytes 884744 | tf_op jit(solution)/shard_map/ppermute | solution.py:118
  152.5 15.9 %collective-permute-start.9 = (f32[48,1536]{1,0:T(8,128)S(1)}, f32[48,1536]{1,0:T(8,128)S(1)}, u32[]{:S(2)}, u32[]{:S(2)}) collective-permute-start(f32[48,1536]{1,0:T(8,128)S(1)} %get-tuple-element.79), channel_id=1, source_target_pairs={{0,0},{1,1},{2,4},{3,5},{4,8},{5,9},{6,12},{7,13},{8,16},{9,17},{1... | collective-permute-start | bytes 884744 | tf_op jit(solution)/shard_map/ppermute | solution.py:118
Sparse Core Ops, SparseCore 0:
  9.7 55.2 all-gather.5
  67.9 85.3 all-gather.3
